TPU v7x, 32 devices: a whole 2x2x4 slice. The times are simulated.
32 devices in a mesh: section: 4 (over x, core), sp: 2 (over y), rep: 4 (over z).
Axes of the slice: x: 2, y: 2, z: 4, core: 2. Of those that a mesh axis runs over, the one named last changes fastest.
Arguments:
- tokens: float32 [2, 2, 24, 3072], P('sp', None, 'section', 'rep'), may hold values from -120 to 120
- mod_scale: float32 [3072], replicated, may hold values from -3 to 3
- mod_shift: float32 [3072], replicated, may hold values from -3 to 3
- proj_weight: float32 [64, 3072], replicated, may hold values from -0.109375 to 0.109375
- proj_bias: float32 [64], replicated, may hold values from -3 to 3
- noisy_latent: float32 [2, 4, 48, 16], P(None, 'sp', 'section'), may hold values from -120 to 120
- in_weight: float32 [3, 3, 3, 16, 512], replicated, may hold values from -0.3125 to 0.3125
- in_bias: float32 [512], replicated, may hold values from -3 to 3
- conv_weight: bfloat16 [3, 3, 3, 256, 512], P(None, None, None, 'rep'), may hold values from -0.0546875 to 0.0546875
- conv_bias: float32 [256], P('rep'), may hold values from -3 to 3
- norm_gain: float32 [256], P('rep'), may hold values from 0.25 to 1.75
- norm_bias: float32 [256], P('rep'), may hold values from -3 to 3
Outputs:
- decoded: float32 [8, 96, 512], P('sp', 'section', 'rep')
All inputs are finite; a program needn't handle non-finite values.
Results may differ from a plain program's by a relative error of at most 0.0026.
Values sent between devices are 32-bit elements; how exact they have to be, the bound alone decides.
No kernel may reach another device: no remote copies, remote signals or barrier semaphores. Data moves between devices by JAX's collectives and lax.ppermute only.
A program may use at most 64 MiB of HBM per device.

v0:
```python
import jax
import jax.numpy as jnp
from jax import lax
from jax.sharding import PartitionSpec as P

D = 3072
LC = 16
CO = 256
GROUPS = 32


def with_halo(block, sides, width):
    for axis, dim in sides:
        count = lax.axis_size(axis)
        forward = [(i, i + 1) for i in range(count - 1)]
        backward = [(target, source) for source, target in forward]
        low = lax.ppermute(
            lax.slice_in_dim(block, block.shape[dim] - width, None, axis=dim), axis, forward
        )
        high = lax.ppermute(lax.slice_in_dim(block, 0, width, axis=dim), axis, backward)
        block = jnp.concatenate([low, block, high], axis=dim)
    return block


def valid_conv(volume, kernel, kernel_spec, precision_mode):
    front = jnp.concatenate([volume[:1], volume[:1], volume], axis=0)
    result = lax.conv_general_dilated(
        front[None],
        kernel,
        (1, 1, 1),
        "VALID",
        dimension_numbers=("NDHWC", kernel_spec, "NDHWC"),
        precision=precision_mode,
        preferred_element_type=jnp.float32,
    )
    return result[0]


def per_device(
    tokens,
    mod_scale,
    mod_shift,
    proj_weight,
    proj_bias,
    noisy_latent,
    in_weight,
    in_bias,
    conv_weight,
    conv_bias,
    norm_gain,
    norm_bias,
):
    local_width = tokens.shape[-1]
    scaled_weight = proj_weight * (1.0 + mod_scale)[None, :]
    center_column = jnp.sum(scaled_weight, axis=1)
    shift_column = (
        jnp.dot(
            proj_weight,
            mod_shift,
            precision=lax.Precision.HIGHEST,
            preferred_element_type=jnp.float32,
        )
        + proj_bias
    )
    local_weight = lax.dynamic_slice_in_dim(
        scaled_weight, lax.axis_index("rep") * local_width, local_width, 1
    )
    moved_tokens = lax.all_to_all(tokens, "sp", split_axis=1, concat_axis=0, tiled=True)
    projected = lax.dot_general(
        moved_tokens,
        local_weight,
        (((3,), (1,)), ((), ())),
        precision=lax.Precision.HIGHEST,
        preferred_element_type=jnp.float32,
    )
    projected, first_sums, square_sums = (
        projected,
        jnp.sum(moved_tokens, axis=-1),
        jnp.sum(moved_tokens * moved_tokens, axis=-1),
    )
    projected, first_sums, square_sums = lax.psum((projected, first_sums, square_sums), "rep")
    token_mean = first_sums / D
    token_var = square_sums / D - token_mean * token_mean
    velocity = (
        lax.rsqrt(token_var + 1e-06)[..., None]
        * (projected - token_mean[..., None] * center_column)
        + shift_column
    )
    frames, slab_rows, band_cols = (velocity.shape[0], velocity.shape[1], velocity.shape[2])
    patches = (
        velocity.reshape(frames, slab_rows, band_cols, LC, 2, 2)
        .transpose(0, 1, 4, 2, 5, 3)
        .reshape(frames, 2 * slab_rows, 2 * band_cols, LC)
    )
    clean = noisy_latent - 0.5 * patches
    extended = with_halo(clean, (("section", 2), ("sp", 1)), 2)
    inner_features = valid_conv(extended, in_weight, "DHWIO", lax.Precision.HIGHEST) + in_bias
    latent_rows = 2 * slab_rows
    latent_cols = 2 * band_cols
    row_global = lax.axis_index("sp") * latent_rows - 1 + jnp.arange(latent_rows + 2)
    col_global = lax.axis_index("section") * latent_cols - 1 + jnp.arange(latent_cols + 2)
    row_inside = (row_global >= 0) & (row_global < latent_rows * lax.axis_size("sp"))
    col_inside = (col_global >= 0) & (col_global < latent_cols * lax.axis_size("section"))
    inside = row_inside[None, :, None, None] & col_inside[None, None, :, None]
    features = jnp.where(inside, inner_features, 0.0).astype(jnp.bfloat16)
    upsampled = jnp.repeat(jnp.repeat(features, 2, axis=1), 2, axis=2)[:, 1:-1, 1:-1, :]
    mixed = valid_conv(upsampled, conv_weight, "DHWOI", None) + conv_bias
    group_size = CO // GROUPS
    local_groups = mixed.shape[-1] // group_size
    grouped = mixed.reshape(-1, local_groups, group_size)
    cell_count = grouped.shape[0] * group_size * lax.axis_size("section") * lax.axis_size("sp")
    group_mean = lax.psum(jnp.sum(grouped, axis=(0, 2)), ("section", "sp")) / cell_count
    deviation = grouped - group_mean[None, :, None]
    group_var = (
        lax.psum(jnp.sum(deviation * deviation, axis=(0, 2)), ("section", "sp")) / cell_count
    )
    normed = (
        (grouped - group_mean[None, :, None]) * lax.rsqrt(group_var + 1e-06)[None, :, None]
    ).reshape(mixed.shape)
    activated = jax.nn.silu(normed * norm_gain + norm_bias)
    out_rows, out_cols, out_chan = (activated.shape[1], activated.shape[2], activated.shape[3])
    return activated.transpose(1, 2, 3, 0).reshape(out_rows, out_cols, out_chan * frames)


def solution(mesh):
    return jax.shard_map(
        per_device,
        mesh=mesh,
        in_specs=(
            P("sp", None, "section", "rep"),
            P(),
            P(),
            P(),
            P(),
            P(None, "sp", "section", None),
            P(),
            P(),
            P(None, None, None, "rep", None),
            P("rep"),
            P("rep"),
            P("rep"),
        ),
        out_specs=P("sp", "section", "rep"),
        check_vma=False,
    )
```

profile of v0, /device:TPU:0, one launch (start us, length us, event | category | flops | bytes accessed | tf_op | source)
XLA Modules:
  0.0 79.5 jit_solution(5452324065720546734)
XLA Ops:
  0.0 0.0 copy-start
  0.0 0.0 copy-start.2
  0.0 1.6 %copy.53 = f32[1,2,6,768]{3,0,2,1:T(1,128)} copy(f32[1,2,6,768]{3,1,2,0:T(2,128)} %param.12) | data formatting | bytes 73728 | tf_op args[0]
  1.6 4.2 %all-to-all-start = ((f32[1,2,6,768]{3,0,2,1:T(1,128)}), f32[1,2,6,768]{3,0,2,1:T(1,128)S(1)}, u32[]{:S(2)}, u32[]{:S(2)}) async-start(f32[1,2,6,768]{3,0,2,1:T(1,128)} %copy.53), calls=%async_computation | async-start | bytes 73728 | tf_op jit(solution)/shard_map/all_to_all | solution.py:68
  5.8 0.7 broadcast_add_fusion
  6.5 1.3 %fusion.37 = (f32[64]{0:T(128)S(1)}, f32[64,3072]{1,0:T(8,128)S(1)}) fusion(f32[64,3072]{1,0:T(8,128)} %param.15, f32[3072]{0:T(1024)S(1)} %broadcast_add_fusion), kind=kLoop, calls=%fused_computation.63 | loop fusion | flops 393152 | bytes 1585408 | tf_op jit(solution)/shard_map/reduce_sum | solution.py:55
  7.9 0.0 copy-start.10
  7.9 0.0 copy-done.1
  7.9 0.0 copy-done.6
  7.9 0.0 copy-done.3
  7.9 0.7 fusion.11
  8.7 1.1 %all-to-all-done = f32[1,2,6,768]{3,0,2,1:T(1,128)S(1)} async-done(((f32[1,2,6,768]{3,0,2,1:T(1,128)}), f32[1,2,6,768]{3,0,2,1:T(1,128)S(1)}, u32[]{:S(2)}, u32[]{:S(2)}) %all-to-all-start) | async-done | bytes 36896 | tf_op jit(solution)/shard_map/all_to_all | solution.py:68
  9.8 0.2 convolution_bitcast_fusion
  10.1 0.2 multiply_reduce_fusion
  10.3 19.4 %all-reduce = (f32[2,1,6,64]{3,2,0,1:T(8,128)S(1)}, f32[2,1,6]{2,0,1:T(2,128)S(1)}, f32[2,1,6]{2,0,1:T(2,128)S(1)}) all-reduce(f32[2,1,6,64]{3,2,0,1:T(8,128)S(1)} %convolution_bitcast_fusion, f32[2,1,6]{2,0,1:T(2,128)S(1)} %bitcast.85, f32[2,1,6]{2,0,1:T(2,128)S(1)} %bitcast.84), channel_id=1, replica_groups=mesh['section'=4,'sp'=2,'rep'=4] {'rep'}, use_global_device_ids=true, to_apply=%region_4.0 | all-reduce | flops 792 | bytes 6336 | tf_op jit(solution)/shard_map/psum | solution.py:81
  29.7 0.1 add_multiply_fusion
  29.8 0.1 copy.56
  29.9 0.1 copy.57
  30.0 0.0 copy-done.2
  30.1 1.3 %collective-permute-start = (f32[2,2,2,16]{3,1,2,0:T(2,128)S(1)}, f32[2,2,2,16]{3,1,2,0:T(2,128)S(1)}, u32[]{:S(2)}, u32[]{:S(2)}) collective-permute-start(f32[2,2,2,16]{3,1,2,0:T(2,128)S(1)} %get-tuple-element.12), channel_id=1, source_target_pairs={{0,8},{8,16},{16,24},{1,9},{9,17},{17,25},{2,10},{10,18},{18,26},{... | collective-permute-start | bytes 1544 | tf_op jit(solution)/shard_map/ppermute | solution.py:17
  31.4 1.3 %collective-permute-start.1 = (f32[2,2,2,16]{3,1,2,0:T(2,128)S(1)}, f32[2,2,2,16]{3,1,2,0:T(2,128)S(1)}, u32[]{:S(2)}, u32[]{:S(2)}) collective-permute-start(f32[2,2,2,16]{3,1,2,0:T(2,128)S(1)} %get-tuple-element.13), channel_id=1, source_target_pairs={{8,0},{16,8},{24,16},{9,1},{17,9},{25,17},{10,2},{18,10},{26,18},{... | collective-permute-start | bytes 1544 | tf_op jit(solution)/shard_map/ppermute | solution.py:20
  32.7 0.0 collective-permute-done
  32.7 3.5 %collective-permute-done.1 = f32[2,2,2,16]{3,1,2,0:T(2,128)S(1)} collective-permute-done((f32[2,2,2,16]{3,1,2,0:T(2,128)S(1)}, f32[2,2,2,16]{3,1,2,0:T(2,128)S(1)}, u32[]{:S(2)}, u32[]{:S(2)}) %collective-permute-start.1) | collective-permute-done | bytes 544 | tf_op jit(solution)/shard_map/ppermute | solution.py:20
  36.2 1.3 %collective-permute-start.3 = (f32[2,2,16,16]{3,1,2,0:T(2,128)S(1)}, f32[2,2,16,16]{3,1,2,0:T(2,128)S(1)}, u32[]{:S(2)}, u32[]{:S(2)}) collective-permute-start(f32[2,2,16,16]{3,1,2,0:T(2,128)S(1)} %pad_maximum_fusion.4), channel_id=1, source_target_pairs={{4,0},{5,1},{6,2},{7,3},{12,8},{13,9},{14,10},{15,11},{20,16},{21,... | collective-permute-start | bytes 12296 | tf_op jit(solution)/shard_map/ppermute | solution.py:20
  37.5 4.5 %collective-permute-start.2 = (f32[2,2,16,16]{3,1,2,0:T(2,128)S(1)}, f32[2,2,16,16]{3,1,2,0:T(2,128)S(1)}, u32[]{:S(2)}, u32[]{:S(2)}) collective-permute-start(f32[2,2,16,16]{3,1,2,0:T(2,128)S(1)} %pad_maximum_fusion.4), channel_id=1, source_target_pairs={{0,4},{1,5},{2,6},{3,7},{8,12},{9,13},{10,14},{11,15},{16,20},{17,... | collective-permute-start | bytes 12296 | tf_op jit(solution)/shard_map/ppermute | solution.py:17
  42.1 0.1 broadcast_and_fusion
  42.1 0.0 collective-permute-done.3
  42.1 1.5 %collective-permute-done.2 = f32[2,2,16,16]{3,1,2,0:T(2,128)S(1)} collective-permute-done((f32[2,2,16,16]{3,1,2,0:T(2,128)S(1)}, f32[2,2,16,16]{3,1,2,0:T(2,128)S(1)}, u32[]{:S(2)}, u32[]{:S(2)}) %collective-permute-start.2) | collective-permute-done | bytes 4128 | tf_op jit(solution)/shard_map/ppermute | solution.py:17
  43.7 0.1 maximum_maximum_fusion
  43.8 0.0 copy-start.4
  43.9 2.8 %convolution_select_fusion = f32[2,4,8,2,512]{4,2,3,1,0:T(8,128)S(1)} fusion(f32[3,3,3,16,512]{4,3,2,1,0:T(8,128)} %param.18, f32[4,6,1,7,2,16]{5,3,4,1,0,2:T(8,128)S(1)} %slice.29, f32[4,6,1,8,2,16]{5,3,4,1,0,2:T(8,128)S(1)} %copy.60, pred[8,2]{0,1:T(4,128)(4,1)S(1)} %copy-done.10), kind=kOutput, calls=%fused_computation.8 | convolution fusion | flops 339841024 | bytes 1192976 | tf_op jit(solution)/shard_map/conv_general_dilated | solution.py:27
  46.7 0.2 copy.61
  46.9 0.1 fusion.19
  47.0 0.1 broadcast_in_dim.23
  47.1 0.1 reshape.129
  47.3 0.1 slice.31
  47.3 0.1 slice.32
  47.4 0.2 maximum_bitcast_fusion
  47.6 0.5 copy.68
  48.1 0.0 copy-start.5
  48.1 0.0 copy-start.9
  48.2 0.3 pad.1.clone
  48.4 0.4 copy.64
  48.9 0.1 slice.33
  49.0 0.0 copy-done
  49.0 0.0 copy-done.5
  49.0 0.0 copy-done.9
  49.0 0.0 copy-start.7
  49.0 0.0 copy-start.8
  49.0 2.0 %select_reduce_fusion.1 = (f32[64]{0:T(128)S(1)}, f32[2,4,8,4,64]{4,2,3,1,0:T(8,128)S(1)}) fusion(f32[64]{0:T(128)S(1)} %copy-done.5, pred[8,4]{0,1:T(4,128)(4,1)S(1)} %copy-done.9, bf16[3,3,3,64,512]{4,3,2,1,0:T(8,128)(2,1)S(1)} %copy-done, bf16[4,6,1,7,2,512]{5,3,4,1,0,2:T(8,128)(2,1)S(1)} %slice.33, bf16[4,6,1,8,4,512]{5,3,4,1,0,2:T(8,128)(2,1)S(1)} %copy.64), kind=kOutput, calls=%fused_computation.31 | convolution fusion | flops 456589248 | bytes 2966048 | tf_op jit(solution)/shard_map/conv_general_dilated | solution.py:27
  51.0 0.1 reduce_sum.69
  51.1 0.1 reduce_sum.70
  51.2 14.4 %psum.38 = f32[8]{0:T(128)S(1)} all-reduce(f32[8]{0:T(128)S(1)} %reduce_sum.70), channel_id=1, replica_groups=mesh['section'=4,'sp'=2,'rep'=4] {'section','sp'}, use_global_device_ids=true, to_apply=%region_8.9 | all-reduce | flops 8 | bytes 64 | tf_op jit(solution)/shard_map/psum | solution.py:112
  65.7 0.1 sub.42
  65.7 0.1 sub.43
  65.8 0.1 select_reduce_fusion
  65.9 0.1 reduce_sum.72
  66.0 0.1 reduce_sum.73
  66.2 12.2 %psum.39 = f32[8]{0:T(128)S(1)} all-reduce(f32[8]{0:T(128)S(1)} %reduce_sum.73), channel_id=1, replica_groups=mesh['section'=4,'sp'=2,'rep'=4] {'section','sp'}, use_global_device_ids=true, to_apply=%region_11.12 | all-reduce | flops 8 | bytes 64 | tf_op jit(solution)/shard_map/psum | solution.py:115
  78.4 0.1 mul.129
  78.5 0.1 mul.130
  78.6 0.1 multiply_bitcast_fusion
  78.7 0.2 copy.66
  78.8 0.7 copy.67
  (22 shorter events, 0.3 us)
Async XLA Ops:
  0.0 49.0 %copy-start = (bf16[3,3,3,64,512]{4,3,2,1,0:T(8,128)(2,1)S(1)}, bf16[3,3,3,64,512]{4,3,2,1,0:T(8,128)(2,1)}, u32[]{:S(2)}) copy-start(bf16[3,3,3,64,512]{4,3,2,1,0:T(8,128)(2,1)} %param.20) | copy-start | bytes 5308420
  0.0 7.9 %copy-start.1 = (f32[64,3072]{1,0:T(8,128)S(1)}, f32[64,3072]{1,0:T(8,128)}, u32[]{:S(2)}) copy-start(f32[64,3072]{1,0:T(8,128)} %param.15) | copy-start | bytes 2359300
  0.0 7.9 %copy-start.6 = (f32[64]{0:T(128)S(1)}, f32[64]{0:T(128)}, u32[]{:S(2)}) copy-start(f32[64]{0:T(128)} %param.16) | copy-start | bytes 772
  0.0 7.9 %copy-start.3 = (f32[3072]{0:T(1024)S(1)}, f32[3072]{0:T(1024)}, u32[]{:S(2)}) copy-start(f32[3072]{0:T(1024)} %param.14) | copy-start | bytes 36868
  0.0 30.0 %copy-start.2 = (f32[2,2,12,16]{3,1,2,0:T(2,128)S(1)}, f32[2,2,12,16]{3,1,2,0:T(2,128)}, u32[]{:S(2)}) copy-start(f32[2,2,12,16]{3,1,2,0:T(2,128)} %param.17) | copy-start | bytes 9220
  1.6 8.2 %all-to-all-start = ((f32[1,2,6,768]{3,0,2,1:T(1,128)}), f32[1,2,6,768]{3,0,2,1:T(1,128)S(1)}, u32[]{:S(2)}, u32[]{:S(2)}) async-start(f32[1,2,6,768]{3,0,2,1:T(1,128)} %copy.53), calls=%async_computation | async-start | bytes 73728 | tf_op jit(solution)/shard_map/all_to_all | solution.py:68
  7.9 36.0 %copy-start.10 = (pred[8,2]{0,1:T(4,128)(4,1)S(1)}, pred[8,2]{0,1:T(4,128)(4,1)}, u32[]{:S(2)}) copy-start(pred[8,2]{0,1:T(4,128)(4,1)} %constant.62) | copy-start | bytes 52
  30.1 2.6 %collective-permute-start = (f32[2,2,2,16]{3,1,2,0:T(2,128)S(1)}, f32[2,2,2,16]{3,1,2,0:T(2,128)S(1)}, u32[]{:S(2)}, u32[]{:S(2)}) collective-permute-start(f32[2,2,2,16]{3,1,2,0:T(2,128)S(1)} %get-tuple-element.12), channel_id=1, source_target_pairs={{0,8},{8,16},{16,24},{1,9},{9,17},{17,25},{2,10},{10,18},{18,26},{... | collective-permute-start | bytes 1544 | tf_op jit(solution)/shard_map/ppermute | solution.py:17
  31.4 4.8 %collective-permute-start.1 = (f32[2,2,2,16]{3,1,2,0:T(2,128)S(1)}, f32[2,2,2,16]{3,1,2,0:T(2,128)S(1)}, u32[]{:S(2)}, u32[]{:S(2)}) collective-permute-start(f32[2,2,2,16]{3,1,2,0:T(2,128)S(1)} %get-tuple-element.13), channel_id=1, source_target_pairs={{8,0},{16,8},{24,16},{9,1},{17,9},{25,17},{10,2},{18,10},{26,18},{... | collective-permute-start | bytes 1544 | tf_op jit(solution)/shard_map/ppermute | solution.py:20
  36.2 5.9 %collective-permute-start.3 = (f32[2,2,16,16]{3,1,2,0:T(2,128)S(1)}, f32[2,2,16,16]{3,1,2,0:T(2,128)S(1)}, u32[]{:S(2)}, u32[]{:S(2)}) collective-permute-start(f32[2,2,16,16]{3,1,2,0:T(2,128)S(1)} %pad_maximum_fusion.4), channel_id=1, source_target_pairs={{4,0},{5,1},{6,2},{7,3},{12,8},{13,9},{14,10},{15,11},{20,16},{21,... | collective-permute-start | bytes 12296 | tf_op jit(solution)/shard_map/ppermute | solution.py:20
  37.5 6.1 %collective-permute-start.2 = (f32[2,2,16,16]{3,1,2,0:T(2,128)S(1)}, f32[2,2,16,16]{3,1,2,0:T(2,128)S(1)}, u32[]{:S(2)}, u32[]{:S(2)}) collective-permute-start(f32[2,2,16,16]{3,1,2,0:T(2,128)S(1)} %pad_maximum_fusion.4), channel_id=1, source_target_pairs={{0,4},{1,5},{2,6},{3,7},{8,12},{9,13},{10,14},{11,15},{16,20},{17,... | collective-permute-start | bytes 12296 | tf_op jit(solution)/shard_map/ppermute | solution.py:17
  43.8 3.0 %copy-start.4 = (f32[512]{0:T(512)S(1)}, f32[512]{0:T(512)}, u32[]{:S(2)}) copy-start(f32[512]{0:T(512)} %param.19) | copy-start | bytes 6148
  48.1 0.9 %copy-start.5 = (f32[64]{0:T(128)S(1)}, f32[64]{0:T(128)}, u32[]{:S(2)}) copy-start(f32[64]{0:T(128)} %param.21) | copy-start | bytes 772
  48.1 0.9 %copy-start.9 = (pred[8,4]{0,1:T(4,128)(4,1)S(1)}, pred[8,4]{0,1:T(4,128)(4,1)}, u32[]{:S(2)}) copy-start(pred[8,4]{0,1:T(4,128)(4,1)} %constant.61) | copy-start | bytes 100
  49.0 29.6 %copy-start.7 = (f32[64]{0:T(128)S(1)}, f32[64]{0:T(128)}, u32[]{:S(2)}) copy-start(f32[64]{0:T(128)} %param.23) | copy-start | bytes 772
  49.0 29.6 %copy-start.8 = (f32[64]{0:T(128)S(1)}, f32[64]{0:T(128)}, u32[]{:S(2)}) copy-start(f32[64]{0:T(128)} %param.22) | copy-start | bytes 772
where the time goes:
time: 80 us; the launch traced here: 79.5 us
  blocking collectives  46.1 us (58%)
  starting transfers between devices  12.7 us (16%)
  waiting for transfers between devices  6.12 us (8%)
  matrix products  5.79 us (7%)
  local copies, waits for them, and re-layouts  5.24 us (7%)
  other arithmetic  3.28 us (4%)
    psum x1, blocking collectives, per_device(): lax.psum((projected, first_sums, square_sums), 'rep')  19.4 us
    psum x1, blocking collectives, per_device(): lax.psum(jnp.sum(grouped, axis=(0, 2)), ('section', 'sp')) / cell_count  14.4 us
    psum x1, blocking collectives, per_device(): lax.psum(jnp.sum(deviation * deviation, axis=(0, 2)), ('section', 'sp'))  12.2 us
    ppermute x2, starting transfers between devices, with_halo(): lax.ppermute(lax.slice_in_dim(block, block.shape[dim] - width, None, axis...  5.84 us
    conv_general_dilated x2, matrix products, valid_conv(): lax.conv_general_dilated(front[None], kernel, (1, 1, 1), 'VALID', dimensi...  4.83 us
    all_to_all x1, starting transfers between devices, per_device(): lax.all_to_all(tokens, 'sp', split_axis=1, concat_axis=0, tiled=True)  4.24 us
    ppermute x2, waiting for transfers between devices, with_halo(): lax.ppermute(lax.slice_in_dim(block, 0, width, axis=dim), axis, backward)  3.47 us
    ppermute x2, starting transfers between devices, with_halo(): lax.ppermute(lax.slice_in_dim(block, 0, width, axis=dim), axis, backward)  2.58 us
  transfers between devices with their start and end apart: 5, of which 3 were waited for; matrix products, arithmetic and copies ran while one was open for 4% of the time, Pallas kernels for 0%

commit v1 on v0

--- a/solution.py
+++ b/solution.py
@@ -112,7 +112,8 @@
     group_mean = lax.psum(jnp.sum(grouped, axis=(0, 2)), ("section", "sp")) / cell_count
     deviation = grouped - group_mean[None, :, None]
     group_var = (
-        lax.psum(jnp.sum(deviation * deviation, axis=(0, 2)), ("section", "sp")) / cell_count
+        lax.psum(lax.psum(jnp.sum(deviation * deviation, axis=(0, 2)), "sp"), "section")
+        / cell_count
     )
     normed = (
         (grouped - group_mean[None, :, None]) * lax.rsqrt(group_var + 1e-06)[None, :, None]

time: 80 us -> 79 us (0.988)
  blocking collectives: 46.1 us -> 45 us
    psum x1 -> x2, blocking collectives: 12.2 us -> 11.2 us  [the longest x1 6.29 us: per_device(): lax.psum(lax.psum(jnp.sum(deviation * deviation, axis=(0, 2)), 'sp'), 'se...]
where the time goes in v1:
time: 79 us; the launch traced here: 78.5 us
  blocking collectives  45 us (57%)
  starting transfers between devices  12.7 us (16%)
  waiting for transfers between devices  6.12 us (8%)
  matrix products  5.79 us (7%)
  local copies, waits for them, and re-layouts  5.23 us (7%)
  other arithmetic  3.28 us (4%)
    psum x1, blocking collectives, per_device(): lax.psum((projected, first_sums, square_sums), 'rep')  19.4 us
    psum x1, blocking collectives, per_device(): lax.psum(jnp.sum(grouped, axis=(0, 2)), ('section', 'sp')) / cell_count  14.4 us
    psum x1, blocking collectives, per_device(): lax.psum(lax.psum(jnp.sum(deviation * deviation, axis=(0, 2)), 'sp'), 'se...  6.29 us
    ppermute x2, starting transfers between devices, with_halo(): lax.ppermute(lax.slice_in_dim(block, block.shape[dim] - width, None, axis...  5.84 us
    psum x1, blocking collectives, per_device(): lax.psum(jnp.sum(deviation * deviation, axis=(0, 2)), 'sp')  4.94 us
    conv_general_dilated x2, matrix products, valid_conv(): lax.conv_general_dilated(front[None], kernel, (1, 1, 1), 'VALID', dimensi...  4.83 us
    all_to_all x1, starting transfers between devices, per_device(): lax.all_to_all(tokens, 'sp', split_axis=1, concat_axis=0, tiled=True)  4.24 us
    ppermute x2, waiting for transfers between devices, with_halo(): lax.ppermute(lax.slice_in_dim(block, 0, width, axis=dim), axis, backward)  3.47 us
  transfers between devices with their start and end apart: 5, of which 3 were waited for; matrix products, arithmetic and copies ran while one was open for 4% of the time, Pallas kernels for 0%

profile of v1, /device:TPU:0, one launch (start us, length us, event | category | flops | bytes accessed | tf_op | source)
XLA Modules:
  0.0 78.5 jit_solution(6929237799358188305)
XLA Ops:
  0.0 0.0 copy-start
  0.0 0.0 copy-start.2
  0.0 1.6 %copy.53 = f32[1,2,6,768]{3,0,2,1:T(1,128)} copy(f32[1,2,6,768]{3,1,2,0:T(2,128)} %param.12) | data formatting | bytes 73728 | tf_op args[0]
  1.6 4.2 %all-to-all-start = ((f32[1,2,6,768]{3,0,2,1:T(1,128)}), f32[1,2,6,768]{3,0,2,1:T(1,128)S(1)}, u32[]{:S(2)}, u32[]{:S(2)}) async-start(f32[1,2,6,768]{3,0,2,1:T(1,128)} %copy.53), calls=%async_computation | async-start | bytes 73728 | tf_op jit(solution)/shard_map/all_to_all | solution.py:68
  5.8 0.7 broadcast_add_fusion
  6.5 1.3 %fusion.37 = (f32[64]{0:T(128)S(1)}, f32[64,3072]{1,0:T(8,128)S(1)}) fusion(f32[64,3072]{1,0:T(8,128)} %param.15, f32[3072]{0:T(1024)S(1)} %broadcast_add_fusion), kind=kLoop, calls=%fused_computation.63 | loop fusion | flops 393152 | bytes 1585408 | tf_op jit(solution)/shard_map/reduce_sum | solution.py:55
  7.9 0.0 copy-start.10
  7.9 0.0 copy-done.1
  7.9 0.0 copy-done.6
  7.9 0.0 copy-done.3
  7.9 0.7 fusion.11
  8.7 1.1 %all-to-all-done = f32[1,2,6,768]{3,0,2,1:T(1,128)S(1)} async-done(((f32[1,2,6,768]{3,0,2,1:T(1,128)}), f32[1,2,6,768]{3,0,2,1:T(1,128)S(1)}, u32[]{:S(2)}, u32[]{:S(2)}) %all-to-all-start) | async-done | bytes 36896 | tf_op jit(solution)/shard_map/all_to_all | solution.py:68
  9.8 0.2 convolution_bitcast_fusion
  10.1 0.2 multiply_reduce_fusion
  10.3 19.4 %all-reduce = (f32[2,1,6,64]{3,2,0,1:T(8,128)S(1)}, f32[2,1,6]{2,0,1:T(2,128)S(1)}, f32[2,1,6]{2,0,1:T(2,128)S(1)}) all-reduce(f32[2,1,6,64]{3,2,0,1:T(8,128)S(1)} %convolution_bitcast_fusion, f32[2,1,6]{2,0,1:T(2,128)S(1)} %bitcast.85, f32[2,1,6]{2,0,1:T(2,128)S(1)} %bitcast.84), channel_id=1, replica_groups=mesh['section'=4,'sp'=2,'rep'=4] {'rep'}, use_global_device_ids=true, to_apply=%region_4.0 | all-reduce | flops 792 | bytes 6336 | tf_op jit(solution)/shard_map/psum | solution.py:81
  29.7 0.1 add_multiply_fusion
  29.8 0.1 copy.56
  29.9 0.1 copy.57
  30.0 0.0 copy-done.2
  30.1 1.3 %collective-permute-start = (f32[2,2,2,16]{3,1,2,0:T(2,128)S(1)}, f32[2,2,2,16]{3,1,2,0:T(2,128)S(1)}, u32[]{:S(2)}, u32[]{:S(2)}) collective-permute-start(f32[2,2,2,16]{3,1,2,0:T(2,128)S(1)} %get-tuple-element.12), channel_id=1, source_target_pairs={{0,8},{8,16},{16,24},{1,9},{9,17},{17,25},{2,10},{10,18},{18,26},{... | collective-permute-start | bytes 1544 | tf_op jit(solution)/shard_map/ppermute | solution.py:17
  31.4 1.3 %collective-permute-start.1 = (f32[2,2,2,16]{3,1,2,0:T(2,128)S(1)}, f32[2,2,2,16]{3,1,2,0:T(2,128)S(1)}, u32[]{:S(2)}, u32[]{:S(2)}) collective-permute-start(f32[2,2,2,16]{3,1,2,0:T(2,128)S(1)} %get-tuple-element.13), channel_id=1, source_target_pairs={{8,0},{16,8},{24,16},{9,1},{17,9},{25,17},{10,2},{18,10},{26,18},{... | collective-permute-start | bytes 1544 | tf_op jit(solution)/shard_map/ppermute | solution.py:20
  32.7 0.0 collective-permute-done
  32.7 3.5 %collective-permute-done.1 = f32[2,2,2,16]{3,1,2,0:T(2,128)S(1)} collective-permute-done((f32[2,2,2,16]{3,1,2,0:T(2,128)S(1)}, f32[2,2,2,16]{3,1,2,0:T(2,128)S(1)}, u32[]{:S(2)}, u32[]{:S(2)}) %collective-permute-start.1) | collective-permute-done | bytes 544 | tf_op jit(solution)/shard_map/ppermute | solution.py:20
  36.2 1.3 %collective-permute-start.3 = (f32[2,2,16,16]{3,1,2,0:T(2,128)S(1)}, f32[2,2,16,16]{3,1,2,0:T(2,128)S(1)}, u32[]{:S(2)}, u32[]{:S(2)}) collective-permute-start(f32[2,2,16,16]{3,1,2,0:T(2,128)S(1)} %pad_maximum_fusion.4), channel_id=1, source_target_pairs={{4,0},{5,1},{6,2},{7,3},{12,8},{13,9},{14,10},{15,11},{20,16},{21,... | collective-permute-start | bytes 12296 | tf_op jit(solution)/shard_map/ppermute | solution.py:20
  37.5 4.5 %collective-permute-start.2 = (f32[2,2,16,16]{3,1,2,0:T(2,128)S(1)}, f32[2,2,16,16]{3,1,2,0:T(2,128)S(1)}, u32[]{:S(2)}, u32[]{:S(2)}) collective-permute-start(f32[2,2,16,16]{3,1,2,0:T(2,128)S(1)} %pad_maximum_fusion.4), channel_id=1, source_target_pairs={{0,4},{1,5},{2,6},{3,7},{8,12},{9,13},{10,14},{11,15},{16,20},{17,... | collective-permute-start | bytes 12296 | tf_op jit(solution)/shard_map/ppermute | solution.py:17
  42.1 0.1 broadcast_and_fusion
  42.1 0.0 collective-permute-done.3
  42.1 1.5 %collective-permute-done.2 = f32[2,2,16,16]{3,1,2,0:T(2,128)S(1)} collective-permute-done((f32[2,2,16,16]{3,1,2,0:T(2,128)S(1)}, f32[2,2,16,16]{3,1,2,0:T(2,128)S(1)}, u32[]{:S(2)}, u32[]{:S(2)}) %collective-permute-start.2) | collective-permute-done | bytes 4128 | tf_op jit(solution)/shard_map/ppermute | solution.py:17
  43.7 0.1 maximum_maximum_fusion
  43.8 0.0 copy-start.4
  43.9 2.8 %convolution_select_fusion = f32[2,4,8,2,512]{4,2,3,1,0:T(8,128)S(1)} fusion(f32[3,3,3,16,512]{4,3,2,1,0:T(8,128)} %param.18, f32[4,6,1,7,2,16]{5,3,4,1,0,2:T(8,128)S(1)} %slice.29, f32[4,6,1,8,2,16]{5,3,4,1,0,2:T(8,128)S(1)} %copy.60, pred[8,2]{0,1:T(4,128)(4,1)S(1)} %copy-done.10), kind=kOutput, calls=%fused_computation.8 | convolution fusion | flops 339841024 | bytes 1192976 | tf_op jit(solution)/shard_map/conv_general_dilated | solution.py:27
  46.7 0.2 copy.61
  46.9 0.1 fusion.19
  47.0 0.1 broadcast_in_dim.23
  47.1 0.1 reshape.129
  47.3 0.1 slice.31
  47.3 0.1 slice.32
  47.4 0.2 maximum_bitcast_fusion
  47.6 0.5 copy.68
  48.1 0.0 copy-start.5
  48.1 0.0 copy-start.9
  48.2 0.3 pad.1.clone
  48.4 0.4 copy.64
  48.9 0.1 slice.33
  49.0 0.0 copy-done
  49.0 0.0 copy-done.5
  49.0 0.0 copy-start.7
  49.0 0.0 copy-start.8
  49.0 2.0 %select_reduce_fusion.1 = (f32[64]{0:T(128)S(1)}, f32[2,4,8,4,64]{4,2,3,1,0:T(8,128)S(1)}) fusion(f32[64]{0:T(128)S(1)} %copy-done.5, pred[8,4]{0,1:T(4,128)(4,1)S(1)} %copy-done.9, bf16[3,3,3,64,512]{4,3,2,1,0:T(8,128)(2,1)S(1)} %copy-done, bf16[4,6,1,7,2,512]{5,3,4,1,0,2:T(8,128)(2,1)S(1)} %slice.33, bf16[4,6,1,8,4,512]{5,3,4,1,0,2:T(8,128)(2,1)S(1)} %copy.64), kind=kOutput, calls=%fused_computation.31 | convolution fusion | flops 456589248 | bytes 2966048 | tf_op jit(solution)/shard_map/conv_general_dilated | solution.py:27
  51.0 0.1 reduce_sum.69
  51.1 0.1 reduce_sum.70
  51.2 14.4 %psum.45 = f32[8]{0:T(128)S(1)} all-reduce(f32[8]{0:T(128)S(1)} %reduce_sum.70), channel_id=1, replica_groups=mesh['section'=4,'sp'=2,'rep'=4] {'section','sp'}, use_global_device_ids=true, to_apply=%region_8.9 | all-reduce | flops 8 | bytes 64 | tf_op jit(solution)/shard_map/psum | solution.py:112
  65.7 0.1 sub.42
  65.7 0.1 sub.43
  65.8 0.1 select_reduce_fusion
  65.9 0.1 reduce_sum.72
  66.0 0.1 reduce_sum.73
  66.1 4.9 %psum.46 = f32[8]{0:T(128)S(1)} all-reduce(f32[8]{0:T(128)S(1)} %reduce_sum.73), channel_id=1, replica_groups=mesh['section'=4,'sp'=2,'rep'=4] {'sp'}, use_global_device_ids=true, to_apply=%region_11.12 | all-reduce | flops 8 | bytes 64 | tf_op jit(solution)/shard_map/psum | solution.py:115
  71.1 6.3 %psum.47 = f32[8]{0:T(128)S(1)} all-reduce(f32[8]{0:T(128)S(1)} %psum.46), channel_id=1, replica_groups=mesh['section'=4,'sp'=2,'rep'=4] {'section'}, use_global_device_ids=true, to_apply=%region_12.13 | all-reduce | flops 8 | bytes 64 | tf_op jit(solution)/shard_map/psum | solution.py:115
  77.4 0.1 mul.129
  77.5 0.1 mul.130
  77.6 0.1 multiply_bitcast_fusion
  77.6 0.2 copy.66
  77.8 0.7 copy.67
  (23 shorter events, 0.3 us)
Async XLA Ops:
  0.0 49.0 %copy-start = (bf16[3,3,3,64,512]{4,3,2,1,0:T(8,128)(2,1)S(1)}, bf16[3,3,3,64,512]{4,3,2,1,0:T(8,128)(2,1)}, u32[]{:S(2)}) copy-start(bf16[3,3,3,64,512]{4,3,2,1,0:T(8,128)(2,1)} %param.20) | copy-start | bytes 5308420
  0.0 7.9 %copy-start.1 = (f32[64,3072]{1,0:T(8,128)S(1)}, f32[64,3072]{1,0:T(8,128)}, u32[]{:S(2)}) copy-start(f32[64,3072]{1,0:T(8,128)} %param.15) | copy-start | bytes 2359300
  0.0 7.9 %copy-start.6 = (f32[64]{0:T(128)S(1)}, f32[64]{0:T(128)}, u32[]{:S(2)}) copy-start(f32[64]{0:T(128)} %param.16) | copy-start | bytes 772
  0.0 7.9 %copy-start.3 = (f32[3072]{0:T(1024)S(1)}, f32[3072]{0:T(1024)}, u32[]{:S(2)}) copy-start(f32[3072]{0:T(1024)} %param.14) | copy-start | bytes 36868
  0.0 30.0 %copy-start.2 = (f32[2,2,12,16]{3,1,2,0:T(2,128)S(1)}, f32[2,2,12,16]{3,1,2,0:T(2,128)}, u32[]{:S(2)}) copy-start(f32[2,2,12,16]{3,1,2,0:T(2,128)} %param.17) | copy-start | bytes 9220
  1.6 8.2 %all-to-all-start = ((f32[1,2,6,768]{3,0,2,1:T(1,128)}), f32[1,2,6,768]{3,0,2,1:T(1,128)S(1)}, u32[]{:S(2)}, u32[]{:S(2)}) async-start(f32[1,2,6,768]{3,0,2,1:T(1,128)} %copy.53), calls=%async_computation | async-start | bytes 73728 | tf_op jit(solution)/shard_map/all_to_all | solution.py:68
  7.9 36.0 %copy-start.10 = (pred[8,2]{0,1:T(4,128)(4,1)S(1)}, pred[8,2]{0,1:T(4,128)(4,1)}, u32[]{:S(2)}) copy-start(pred[8,2]{0,1:T(4,128)(4,1)} %constant.62) | copy-start | bytes 52
  30.1 2.6 %collective-permute-start = (f32[2,2,2,16]{3,1,2,0:T(2,128)S(1)}, f32[2,2,2,16]{3,1,2,0:T(2,128)S(1)}, u32[]{:S(2)}, u32[]{:S(2)}) collective-permute-start(f32[2,2,2,16]{3,1,2,0:T(2,128)S(1)} %get-tuple-element.12), channel_id=1, source_target_pairs={{0,8},{8,16},{16,24},{1,9},{9,17},{17,25},{2,10},{10,18},{18,26},{... | collective-permute-start | bytes 1544 | tf_op jit(solution)/shard_map/ppermute | solution.py:17
  31.4 4.8 %collective-permute-start.1 = (f32[2,2,2,16]{3,1,2,0:T(2,128)S(1)}, f32[2,2,2,16]{3,1,2,0:T(2,128)S(1)}, u32[]{:S(2)}, u32[]{:S(2)}) collective-permute-start(f32[2,2,2,16]{3,1,2,0:T(2,128)S(1)} %get-tuple-element.13), channel_id=1, source_target_pairs={{8,0},{16,8},{24,16},{9,1},{17,9},{25,17},{10,2},{18,10},{26,18},{... | collective-permute-start | bytes 1544 | tf_op jit(solution)/shard_map/ppermute | solution.py:20
  36.2 5.9 %collective-permute-start.3 = (f32[2,2,16,16]{3,1,2,0:T(2,128)S(1)}, f32[2,2,16,16]{3,1,2,0:T(2,128)S(1)}, u32[]{:S(2)}, u32[]{:S(2)}) collective-permute-start(f32[2,2,16,16]{3,1,2,0:T(2,128)S(1)} %pad_maximum_fusion.4), channel_id=1, source_target_pairs={{4,0},{5,1},{6,2},{7,3},{12,8},{13,9},{14,10},{15,11},{20,16},{21,... | collective-permute-start | bytes 12296 | tf_op jit(solution)/shard_map/ppermute | solution.py:20
  37.5 6.1 %collective-permute-start.2 = (f32[2,2,16,16]{3,1,2,0:T(2,128)S(1)}, f32[2,2,16,16]{3,1,2,0:T(2,128)S(1)}, u32[]{:S(2)}, u32[]{:S(2)}) collective-permute-start(f32[2,2,16,16]{3,1,2,0:T(2,128)S(1)} %pad_maximum_fusion.4), channel_id=1, source_target_pairs={{0,4},{1,5},{2,6},{3,7},{8,12},{9,13},{10,14},{11,15},{16,20},{17,... | collective-permute-start | bytes 12296 | tf_op jit(solution)/shard_map/ppermute | solution.py:17
  43.8 3.0 %copy-start.4 = (f32[512]{0:T(512)S(1)}, f32[512]{0:T(512)}, u32[]{:S(2)}) copy-start(f32[512]{0:T(512)} %param.19) | copy-start | bytes 6148
  48.1 0.9 %copy-start.5 = (f32[64]{0:T(128)S(1)}, f32[64]{0:T(128)}, u32[]{:S(2)}) copy-start(f32[64]{0:T(128)} %param.21) | copy-start | bytes 772
  48.1 0.9 %copy-start.9 = (pred[8,4]{0,1:T(4,128)(4,1)S(1)}, pred[8,4]{0,1:T(4,128)(4,1)}, u32[]{:S(2)}) copy-start(pred[8,4]{0,1:T(4,128)(4,1)} %constant.61) | copy-start | bytes 100
  49.0 28.6 %copy-start.7 = (f32[64]{0:T(128)S(1)}, f32[64]{0:T(128)}, u32[]{:S(2)}) copy-start(f32[64]{0:T(128)} %param.23) | copy-start | bytes 772
  49.0 28.5 %copy-start.8 = (f32[64]{0:T(128)S(1)}, f32[64]{0:T(128)}, u32[]{:S(2)}) copy-start(f32[64]{0:T(128)} %param.22) | copy-start | bytes 772
